TPU v7x, 128 devices: a whole 4x4x4 slice. The times are simulated.
128 devices in a mesh: segment: 4 (over z), latent: 8 (over y_hi, x), tok: 4 (over y_lo, core).
Axes of the slice: x: 4, y: 4 (y_hi: 2, y_lo: 2; y = y_hi * 2 + y_lo), z: 4, core: 2. Of those that a mesh axis runs over, the one named last changes fastest.
Arguments:
- window: bfloat16 [512, 2304], P('tok'), may hold values from -8 to 8
- norm_gain: float32 [4, 2304], P('segment'), may hold values from 0.25 to 1.75
- enc_weight: bfloat16 [4, 2304, 65536], P('segment', None, ('latent', 'tok')), may hold values from -0.125 to 0.125
- enc_bias: float32 [4, 65536], P('segment', ('latent', 'tok')), may hold values from -1.5 to 1.5
- thresholds: int32 [4, 65536], P('segment', ('latent', 'tok')), may hold values from 256 to 1535
- dec_weight: bfloat16 [4, 65536, 2304], P('segment', ('latent', 'tok')), may hold values from -0.046875 to 0.046875
- dec_bias: float32 [4, 2304], P('segment'), may hold values from -2.5 to 2.5
- rates_start: float32 [4, 65536], P('segment', ('latent', 'tok')), may hold values from 0 to 1
- block_order: int32 [4, 8], P('segment'), may hold values from 0 to 7, each once within a row
Outputs:
- layer_out: bfloat16 [4, 512, 2304], P('segment', 'tok')
- latent_act: bfloat16 [4, 512, 65536], P('segment', None, ('latent', 'tok'))
- recon: bfloat16 [4, 512, 2304], P('segment', 'tok')
- rates: float32 [4, 65536], P('segment', ('latent', 'tok'))
All inputs are finite; a program needn't handle non-finite values.
Results may differ from a plain program's by a relative error of at most 0.014.
Values may be sent and summed in bfloat16 or wider, within the bound.
No kernel may reach another device: no remote copies, remote signals or barrier semaphores. Data moves between devices by JAX's collectives and lax.ppermute only.
A program may use at most 128 MiB of HBM per device.

v0:
```python
import jax
import jax.numpy as jnp
from jax import lax
from jax.sharding import PartitionSpec as P

ROWS_DEV = 128
MICRO = 8
BLOCKS = 8


EPSILON = 1e-06
SHARPNESS = 20.0
RATE_DECAY = 0.8


def from_behind(array, axis, by):
    devices = lax.axis_size(axis)
    pairs = [(i, i + by) for i in range(devices) if 0 <= i + by < devices]
    return lax.ppermute(array, axis, pairs)


def per_device(
    window,
    norm_gain,
    enc_weight,
    enc_bias,
    thresholds,
    dec_weight,
    dec_bias,
    rates_start,
    block_order,
):
    tok_count = lax.axis_size("tok")
    my_index = lax.axis_index("tok")
    segment_count = lax.axis_size("segment")
    segment_index = lax.axis_index("segment")
    local_rows = ROWS_DEV // MICRO
    width = window.shape[1]
    encoder = enc_weight[0]
    decoder = dec_weight[0]
    lat_local = encoder.shape[1]
    gain_row = norm_gain[0][None, :]
    enc_row = enc_bias[0][None, :]
    theta_row = thresholds[0].astype(jnp.float32)[None, :] / 1024.0
    dec_row = dec_bias[0][None, :]
    all_rows = ROWS_DEV * tok_count
    block_rows = all_rows // BLOCKS
    onehot = (block_order[0][:, None] == jnp.arange(BLOCKS, dtype=jnp.int32)[None, :]).astype(
        jnp.float32
    )
    position = jnp.dot(
        jnp.arange(BLOCKS).astype(jnp.float32), onehot, precision=lax.Precision.HIGHEST
    )
    block_weight = (1.0 - RATE_DECAY) * jnp.power(jnp.float32(RATE_DECAY), BLOCKS - 1.0 - position)
    row_weight = jnp.repeat(block_weight / block_rows, block_rows).reshape(
        tok_count, MICRO, local_rows
    )
    carried = jnp.zeros((local_rows, width), jnp.bfloat16)
    layer_buf = jnp.zeros((ROWS_DEV, width), jnp.bfloat16)
    recon_buf = jnp.zeros((ROWS_DEV, width), jnp.bfloat16)
    latent_buf = jnp.zeros((tok_count, MICRO, local_rows, lat_local), jnp.bfloat16)
    rate_acc = jnp.zeros((lat_local,), jnp.float32)
    for tick in range(MICRO + segment_count - 1):
        micro_here = tick - segment_index
        valid = jnp.logical_and(micro_here >= 0, micro_here < MICRO)
        micro_idx = jnp.clip(micro_here, 0, MICRO - 1)
        if tick < MICRO:
            fresh = window[tick * local_rows : (tick + 1) * local_rows]
        else:
            fresh = jnp.zeros((local_rows, width), jnp.bfloat16)
        incoming = jnp.where(segment_index == 0, fresh, carried)
        hidden = incoming.astype(jnp.float32)
        scale = lax.rsqrt(jnp.mean(hidden * hidden, axis=-1, keepdims=True) + EPSILON)
        normed = (hidden * scale * gain_row).astype(jnp.bfloat16)
        pre_act = (
            jnp.dot(
                lax.all_gather(normed, "tok", axis=0, tiled=True),
                encoder,
                preferred_element_type=jnp.float32,
            )
            + enc_row
        )
        fire_gate = jax.nn.sigmoid(SHARPNESS * (pre_act - theta_row))
        latents = (pre_act * fire_gate).astype(jnp.bfloat16)
        weights_now = lax.dynamic_slice(
            row_weight, (0, micro_idx, 0), (tok_count, 1, local_rows)
        ).reshape(-1)
        rate_term = jnp.dot(weights_now, fire_gate, precision=lax.Precision.HIGHEST)
        rate_acc = rate_acc + jnp.where(valid, rate_term, 0.0)
        latent_grid = latents.reshape(tok_count, 1, local_rows, lat_local)
        previous = lax.dynamic_slice(
            latent_buf, (0, micro_idx, 0, 0), (tok_count, 1, local_rows, lat_local)
        )
        latent_buf = lax.dynamic_update_slice(
            latent_buf, jnp.where(valid, latent_grid, previous), (0, micro_idx, 0, 0)
        )
        partial_sum = jnp.dot(latents, decoder, preferred_element_type=jnp.float32)
        summed = lax.psum(partial_sum, ("latent", "tok"))
        mine = lax.dynamic_slice_in_dim(summed, my_index * local_rows, local_rows, 0)
        recon_sum = mine + dec_row
        layer = (hidden + recon_sum).astype(jnp.bfloat16)
        recon_now = recon_sum.astype(jnp.bfloat16)
        row_start = micro_idx * local_rows
        old_layer = lax.dynamic_slice_in_dim(layer_buf, row_start, local_rows, 0)
        layer_buf = lax.dynamic_update_slice_in_dim(
            layer_buf, jnp.where(valid, layer, old_layer), row_start, 0
        )
        old_recon = lax.dynamic_slice_in_dim(recon_buf, row_start, local_rows, 0)
        recon_buf = lax.dynamic_update_slice_in_dim(
            recon_buf, jnp.where(valid, recon_now, old_recon), row_start, 0
        )
        carried = from_behind(layer, "segment", 1)
    final_rates = RATE_DECAY**BLOCKS * rates_start[0] + rate_acc
    latent_out = latent_buf.reshape(tok_count * ROWS_DEV, lat_local)
    return (layer_buf[None], latent_out[None], recon_buf[None], final_rates[None])


def solution(mesh):
    placed = (
        P("tok", None),
        P("segment", None),
        P("segment", None, ("latent", "tok")),
        P("segment", ("latent", "tok")),
        P("segment", ("latent", "tok")),
        P("segment", ("latent", "tok"), None),
        P("segment", None),
        P("segment", ("latent", "tok")),
        P("segment", None),
    )
    return jax.shard_map(
        per_device,
        mesh=mesh,
        in_specs=placed,
        out_specs=(
            P("segment", "tok", None),
            P("segment", None, ("latent", "tok")),
            P("segment", "tok", None),
            P("segment", ("latent", "tok")),
        ),
        check_vma=False,
    )
```

profile of v0, /device:TPU:64, one launch (start us, length us, event | category | flops | bytes accessed | tf_op | source)
XLA Modules:
  0.0 1402.8 jit_solution(11238650662855236594)
XLA Ops:
  10.8 6.0 all_gather.33
  35.0 94.8 %all-reduce.12.cloned.1.call-done = f32[64,2304]{1,0:T(8,128)} async-done(((f32[64,2304]{1,0:T(8,128)}), f32[64,2304]{1,0:T(8,128)}) %all-reduce.12.cloned.1.call-update) | async-done | bytes 589840 | tf_op jit(solution)/shard_map/psum | solution.py:98
  138.8 5.9 all_gather.34
  144.7 6.5 multiply_convert_fusion.9
  153.9 102.1 %all-reduce.14.cloned.1.call-done = f32[64,2304]{1,0:T(8,128)} async-done(((f32[64,2304]{1,0:T(8,128)}), f32[64,2304]{1,0:T(8,128)}) %all-reduce.14.cloned.1.call-update) | async-done | bytes 589840 | tf_op jit(solution)/shard_map/psum | solution.py:98
  265.4 5.9 all_gather.35
  271.3 6.5 multiply_convert_fusion.8
  280.5 102.1 %all-reduce.16.cloned.1.call-done = f32[64,2304]{1,0:T(8,128)} async-done(((f32[64,2304]{1,0:T(8,128)}), f32[64,2304]{1,0:T(8,128)}) %all-reduce.16.cloned.1.call-update) | async-done | bytes 589840 | tf_op jit(solution)/shard_map/psum | solution.py:98
  392.0 5.9 all_gather.36
  397.9 6.5 multiply_convert_fusion.7
  407.1 102.2 %all-reduce.18.cloned.1.call-done = f32[64,2304]{1,0:T(8,128)} async-done(((f32[64,2304]{1,0:T(8,128)}), f32[64,2304]{1,0:T(8,128)}) %all-reduce.18.cloned.1.call-update) | async-done | bytes 589840 | tf_op jit(solution)/shard_map/psum | solution.py:98
  518.7 5.9 all_gather.37
  524.5 6.5 multiply_convert_fusion.6
  533.7 102.2 %all-reduce.20.cloned.1.call-done = f32[64,2304]{1,0:T(8,128)} async-done(((f32[64,2304]{1,0:T(8,128)}), f32[64,2304]{1,0:T(8,128)}) %all-reduce.20.cloned.1.call-update) | async-done | bytes 589840 | tf_op jit(solution)/shard_map/psum | solution.py:98
  645.3 5.9 all_gather.38
  651.2 6.5 multiply_convert_fusion.5
  660.4 102.1 %all-reduce.22.cloned.1.call-done = f32[64,2304]{1,0:T(8,128)} async-done(((f32[64,2304]{1,0:T(8,128)}), f32[64,2304]{1,0:T(8,128)}) %all-reduce.22.cloned.1.call-update) | async-done | bytes 589840 | tf_op jit(solution)/shard_map/psum | solution.py:98
  771.9 6.0 all_gather.39
  778.0 6.5 multiply_convert_fusion.4
  787.2 102.1 %all-reduce.24.cloned.1.call-done = f32[64,2304]{1,0:T(8,128)} async-done(((f32[64,2304]{1,0:T(8,128)}), f32[64,2304]{1,0:T(8,128)}) %all-reduce.24.cloned.1.call-update) | async-done | bytes 589840 | tf_op jit(solution)/shard_map/psum | solution.py:98
  898.7 5.9 all_gather.40
  904.6 6.5 multiply_convert_fusion.3
  913.8 102.1 %all-reduce.26.cloned.1.call-done = f32[64,2304]{1,0:T(8,128)} async-done(((f32[64,2304]{1,0:T(8,128)}), f32[64,2304]{1,0:T(8,128)}) %all-reduce.26.cloned.1.call-update) | async-done | bytes 589840 | tf_op jit(solution)/shard_map/psum | solution.py:98
  1024.3 5.9 all_gather.41
  1030.2 6.5 multiply_convert_fusion.2
  1039.4 102.2 %all-reduce.28.cloned.1.call-done = f32[64,2304]{1,0:T(8,128)} async-done(((f32[64,2304]{1,0:T(8,128)}), f32[64,2304]{1,0:T(8,128)}) %all-reduce.28.cloned.1.call-update) | async-done | bytes 589840 | tf_op jit(solution)/shard_map/psum | solution.py:98
  1149.9 6.1 all_gather.42
  1156.0 6.5 multiply_convert_fusion.1
  1165.2 102.2 %all-reduce.30.cloned.1.call-done = f32[64,2304]{1,0:T(8,128)} async-done(((f32[64,2304]{1,0:T(8,128)}), f32[64,2304]{1,0:T(8,128)}) %all-reduce.30.cloned.1.call-update) | async-done | bytes 589840 | tf_op jit(solution)/shard_map/psum | solution.py:98
  1276.5 6.0 all_gather.43
  1282.5 6.5 multiply_convert_fusion
  1296.1 98.3 %all-reduce.32.cloned.1.call-done = f32[64,2304]{1,0:T(8,128)} async-done(((f32[64,2304]{1,0:T(8,128)}), f32[64,2304]{1,0:T(8,128)}) %all-reduce.32.cloned.1.call-update) | async-done | bytes 589840 | tf_op jit(solution)/shard_map/psum | solution.py:98
  (266 shorter events, 145.4 us)
Async XLA Ops:
  7.2 122.7 %all-reduce.12.cloned.1.call-start = ((), (), s32[]{:S(2)}) async-start(), calls=%async_computation | async-start | bytes 1179648 | tf_op jit(solution)/shard_map/psum | solution.py:98
  9.0 129.4 %copy-start.1 = (f32[1,2048]{1,0:T(1,128)}, f32[1,2048]{1,0:T(1,128)S(1)}, u32[]{:S(2)}) copy-start(f32[1,2048]{1,0:T(1,128)S(1)} %convert_multiply_fusion.22) | copy-start | bytes 24580
  9.7 128.6 %copy-start = (f32[2304]{0:T(1024)}, f32[2304]{0:T(1024)S(1)}, u32[]{:S(2)}) copy-start(f32[2304]{0:T(1024)S(1)} %reduce) | copy-start | bytes 27652
  25.5 230.5 %all-reduce.14.cloned.1.call-start = ((), (), s32[]{:S(2)}) async-start(), calls=%async_computation.1 | async-start | bytes 1179648 | tf_op jit(solution)/shard_map/psum | solution.py:98
  130.9 6.2 collective-permute-start
  135.1 16.1 %slice-start.3 = ((s8[9437184]{0:T(1024)(128)(4,1)}), s8[4194304]{0:T(1024)(128)(4,1)S(1)}, s32[]{:S(2)}) async-start(s8[9437184]{0:T(1024)(128)(4,1)} %bitcast.196), calls=%async_computation.14 | async-start | bytes 8388608
  153.8 228.9 %all-reduce.16.cloned.1.call-start = ((), (), s32[]{:S(2)}) async-start(), calls=%async_computation.2 | async-start | bytes 1179648 | tf_op jit(solution)/shard_map/psum | solution.py:98
  257.0 6.2 collective-permute-start.1
  262.3 15.5 %slice-start.6 = ((s8[9437184]{0:T(1024)(128)(4,1)}), s8[4194304]{0:T(1024)(128)(4,1)S(1)}, s32[]{:S(2)}) async-start(s8[9437184]{0:T(1024)(128)(4,1)} %bitcast.198), calls=%async_computation.17 | async-start | bytes 8388608
  280.4 228.9 %all-reduce.18.cloned.1.call-start = ((), (), s32[]{:S(2)}) async-start(), calls=%async_computation.3 | async-start | bytes 1179648 | tf_op jit(solution)/shard_map/psum | solution.py:98
  383.6 6.2 collective-permute-start.2
  389.4 15.0 %slice-start.9 = ((s8[9437184]{0:T(1024)(128)(4,1)}), s8[4194304]{0:T(1024)(128)(4,1)S(1)}, s32[]{:S(2)}) async-start(s8[9437184]{0:T(1024)(128)(4,1)} %bitcast.200), calls=%async_computation.20 | async-start | bytes 8388608
  407.0 228.9 %all-reduce.20.cloned.1.call-start = ((), (), s32[]{:S(2)}) async-start(), calls=%async_computation.4 | async-start | bytes 1179648 | tf_op jit(solution)/shard_map/psum | solution.py:98
  510.3 6.2 collective-permute-start.3
  515.5 15.5 %slice-start.12 = ((s8[9437184]{0:T(1024)(128)(4,1)}), s8[4194304]{0:T(1024)(128)(4,1)S(1)}, s32[]{:S(2)}) async-start(s8[9437184]{0:T(1024)(128)(4,1)} %bitcast.202), calls=%async_computation.23 | async-start | bytes 8388608
  533.6 228.9 %all-reduce.22.cloned.1.call-start = ((), (), s32[]{:S(2)}) async-start(), calls=%async_computation.5 | async-start | bytes 1179648 | tf_op jit(solution)/shard_map/psum | solution.py:98
  636.9 6.2 collective-permute-start.4
  642.2 15.5 %slice-start.15 = ((s8[9437184]{0:T(1024)(128)(4,1)}), s8[4194304]{0:T(1024)(128)(4,1)S(1)}, s32[]{:S(2)}) async-start(s8[9437184]{0:T(1024)(128)(4,1)} %bitcast.204), calls=%async_computation.26 | async-start | bytes 8388608
  660.3 229.0 %all-reduce.24.cloned.1.call-start = ((), (), s32[]{:S(2)}) async-start(), calls=%async_computation.6 | async-start | bytes 1179648 | tf_op jit(solution)/shard_map/psum | solution.py:98
  763.5 6.2 collective-permute-start.5
  768.8 15.7 %slice-start.18 = ((s8[9437184]{0:T(1024)(128)(4,1)}), s8[4194304]{0:T(1024)(128)(4,1)S(1)}, s32[]{:S(2)}) async-start(s8[9437184]{0:T(1024)(128)(4,1)} %bitcast.206), calls=%async_computation.29 | async-start | bytes 8388608
  787.1 228.9 %all-reduce.26.cloned.1.call-start = ((), (), s32[]{:S(2)}) async-start(), calls=%async_computation.7 | async-start | bytes 1179648 | tf_op jit(solution)/shard_map/psum | solution.py:98
  890.3 6.2 collective-permute-start.6
  895.6 15.5 %slice-start.21 = ((s8[9437184]{0:T(1024)(128)(4,1)}), s8[4194304]{0:T(1024)(128)(4,1)S(1)}, s32[]{:S(2)}) async-start(s8[9437184]{0:T(1024)(128)(4,1)} %bitcast.208), calls=%async_computation.32 | async-start | bytes 8388608
  913.7 227.9 %all-reduce.28.cloned.1.call-start = ((), (), s32[]{:S(2)}) async-start(), calls=%async_computation.8 | async-start | bytes 1179648 | tf_op jit(solution)/shard_map/psum | solution.py:98
  1016.9 6.2 collective-permute-start.7
  1022.2 14.5 %slice-start.24 = ((s8[9437184]{0:T(1024)(128)(4,1)}), s8[4194304]{0:T(1024)(128)(4,1)S(1)}, s32[]{:S(2)}) async-start(s8[9437184]{0:T(1024)(128)(4,1)} %bitcast.210), calls=%async_computation.35 | async-start | bytes 8388608
  1039.3 228.2 %all-reduce.30.cloned.1.call-start = ((), (), s32[]{:S(2)}) async-start(), calls=%async_computation.9 | async-start | bytes 1179648 | tf_op jit(solution)/shard_map/psum | solution.py:98
  1142.6 6.2 collective-permute-start.8
  1147.9 14.7 %slice-start.27 = ((s8[9437184]{0:T(1024)(128)(4,1)}), s8[4194304]{0:T(1024)(128)(4,1)S(1)}, s32[]{:S(2)}) async-start(s8[9437184]{0:T(1024)(128)(4,1)} %bitcast.212), calls=%async_computation.38 | async-start | bytes 8388608
  1165.1 229.2 %all-reduce.32.cloned.1.call-start = ((), (), s32[]{:S(2)}) async-start(), calls=%async_computation.10 | async-start | bytes 1179648 | tf_op jit(solution)/shard_map/psum | solution.py:98
  1268.4 6.9 collective-permute-start.9
  (37 other events, 194.9 us)
Sparse Core Ops, SparseCore 0:
  25.7 104.1 all-reduce.11
  153.9 102.0 all-reduce.13
  280.5 102.0 all-reduce.15
  407.1 102.1 all-reduce.17
  533.7 102.1 all-reduce.19
  660.4 102.0 all-reduce.21
  787.2 102.0 all-reduce.23
  913.8 102.0 all-reduce.25
  1039.4 102.1 all-reduce.27
  1165.2 102.1 all-reduce.29
  1291.7 102.6 all-reduce.31
where the time goes:
time: 1410 us; the launch traced here: 1400 us
  waiting for transfers between devices  1120 us (79%)
  matrix products  120 us (9%)
  blocking collectives  65.2 us (5%)
  other arithmetic  36.1 us (3%)
  starting transfers between devices  32.6 us (2%)
  between operations  14.8 us (1%)
    psum x11, waiting for transfers between devices, per_device(): summed = lax.psum(partial_sum, ('latent', 'tok'))  1110 us
    dot_general x11, matrix products, per_device(): jnp.dot(lax.all_gather(normed, 'tok', axis=0, tiled=True), encoder, prefe...  70.6 us
    all_gather x11, blocking collectives, per_device(): lax.all_gather(normed, 'tok', axis=0, tiled=True)  65.2 us
    ppermute x10, starting transfers between devices, from_behind(): return lax.ppermute(array, axis, pairs)  32.1 us
  transfers between devices with their start and end apart: 21, of which 20 were waited for; matrix products, arithmetic and copies ran while one was open for 3% of the time, Pallas kernels for 0%

commit v1 on v0

--- a/solution.py
+++ b/solution.py
@@ -17,6 +17,28 @@
     devices = lax.axis_size(axis)
     pairs = [(i, i + by) for i in range(devices) if 0 <= i + by < devices]
     return lax.ppermute(array, axis, pairs)
+
+
+def swap_with(array, axis, bit):
+    devices = lax.axis_size(axis)
+    return lax.ppermute(array, axis, [(i, i ^ bit) for i in range(devices)])
+
+
+def reduce_rows(partial_sum, local_rows):
+    width = partial_sum.shape[1]
+    tok_index = lax.axis_index("tok")
+    core = tok_index % 2
+    low = tok_index // 2
+    blocks = partial_sum.reshape(2, 2, local_rows, width)
+    keep = lax.dynamic_index_in_dim(blocks, core, axis=1, keepdims=False)
+    send = lax.dynamic_index_in_dim(blocks, 1 - core, axis=1, keepdims=False)
+    halves = keep + swap_with(send, "tok", 1)
+    keep = lax.dynamic_index_in_dim(halves, low, axis=0, keepdims=False)
+    send = lax.dynamic_index_in_dim(halves, 1 - low, axis=0, keepdims=False)
+    total = keep + swap_with(send, "tok", 2)
+    for bit in (4, 1, 2):
+        total = total + swap_with(total, "latent", bit)
+    return total
 
 
 def per_device(
@@ -95,8 +117,7 @@
             latent_buf, jnp.where(valid, latent_grid, previous), (0, micro_idx, 0, 0)
         )
         partial_sum = jnp.dot(latents, decoder, preferred_element_type=jnp.float32)
-        summed = lax.psum(partial_sum, ("latent", "tok"))
-        mine = lax.dynamic_slice_in_dim(summed, my_index * local_rows, local_rows, 0)
+        mine = reduce_rows(partial_sum, local_rows)
         recon_sum = mine + dec_row
         layer = (hidden + recon_sum).astype(jnp.bfloat16)
         recon_now = recon_sum.astype(jnp.bfloat16)

time: 1410 us -> 542 us (0.38)
  waiting for transfers between devices: 1120 us -> 194 us
  starting transfers between devices: 32.6 us -> 164 us
  matrix products: 120 us -> 87.4 us
  other arithmetic: 36.1 us -> 12.6 us
    psum x11 -> x0, waiting for transfers between devices: 1110 us -> none  [per_device(): summed = lax.psum(partial_sum, ('latent', 'tok'))]
    ppermute x0 -> x55, waiting for transfers between devices: none -> 169 us  [swap_with(): return lax.ppermute(array, axis, [(i, i ^ bit) for i in range(devices)])]
    ppermute x0 -> x55, starting transfers between devices: none -> 127 us  [swap_with(): return lax.ppermute(array, axis, [(i, i ^ bit) for i in range(devices)])]
    ppermute x10, waiting for transfers between devices: 9.38 us -> 25.7 us  [from_behind(): return lax.ppermute(array, axis, pairs)]
    dot_general x11, matrix products: 21.4 us -> 7.22 us  [per_device(): rate_term = jnp.dot(weights_now, fire_gate, precision=lax.Precision.HIGHEST)]
  transfers between devices with their start and end apart: 21 -> 65, of which waited for: 20 -> 64; matrix products, arithmetic and copies ran while one was open for 3% -> 2% of each run, Pallas kernels for 0% -> 0%
where the time goes in v1:
time: 542 us; the launch traced here: 533 us
  waiting for transfers between devices  194 us (36%)
  starting transfers between devices  164 us (30%)
  matrix products  87.4 us (16%)
  blocking collectives  65.4 us (12%)
  other arithmetic  12.6 us (2%)
  local copies, waits for them, and re-layouts  7.44 us (1%)
    ppermute x55, waiting for transfers between devices, swap_with(): return lax.ppermute(array, axis, [(i, i ^ bit) for i in range(devices)])  169 us
    ppermute x55, starting transfers between devices, swap_with(): return lax.ppermute(array, axis, [(i, i ^ bit) for i in range(devices)])  127 us
    all_gather x11, blocking collectives, per_device(): lax.all_gather(normed, 'tok', axis=0, tiled=True)  65.4 us
    dot_general x11, matrix products, per_device(): jnp.dot(lax.all_gather(normed, 'tok', axis=0, tiled=True), encoder, prefe...  61.1 us
    ppermute x10, starting transfers between devices, from_behind(): return lax.ppermute(array, axis, pairs)  37.4 us
    ppermute x10, waiting for transfers between devices, from_behind(): return lax.ppermute(array, axis, pairs)  25.7 us
    dot_general x11, matrix products, per_device(): partial_sum = jnp.dot(latents, decoder, preferred_element_type=jnp.float32)  18.9 us
  transfers between devices with their start and end apart: 65, of which 64 were waited for; matrix products, arithmetic and copies ran while one was open for 2% of the time, Pallas kernels for 0%

profile of v1, /device:TPU:64, one launch (start us, length us, event | category | flops | bytes accessed | tf_op | source)
XLA Modules:
  0.0 533.2 jit_solution(3653518175072138877)
XLA Ops:
  4.2 6.0 %all_gather.33 = bf16[64,2304]{1,0:T(8,128)(2,1)S(1)} all-gather(bf16[16,2304]{1,0:T(8,128)(2,1)S(1)} %fusion.126), channel_id=1, replica_groups=mesh['segment'=4,'latent'=8,'tok'=4] {'tok'}, dimensions={0}, use_global_device_ids=true | all-gather | bytes 368640 | tf_op jit(solution)/shard_map/all_gather | solution.py:99
  10.2 6.5 %broadcast_select_fusion = (bf16[64,2048]{1,0:T(8,128)(2,1)S(1)}, bf16[64,2048]{1,0:T(8,128)(2,1)S(1)}, f32[64,2048]{1,0:T(8,128)}) fusion(pred[]{:T(512)S(6)} %and.65, f32[2048]{0:T(1024)S(1)} %bitcast.339, f32[2048]{0:T(1024)} %bitcast.362, bf16[64,2304]{1,0:T(8,128)(2,1)S(1)} %all_gather.33, bf16[1,2304,2048]{2,1,0:T(8,128)(2,1)} %param.11), kind=kOutput, calls=%fused_computation.157 | convolution fusion | flops 605159424 | bytes 10797057 | tf_op jit(solution)/shard_map/dot_general | solution.py:98
  52.1 5.9 %all_gather.34 = bf16[64,2304]{1,0:T(8,128)(2,1)S(1)} all-gather(bf16[16,2304]{1,0:T(8,128)(2,1)S(1)} %fusion.130), channel_id=1, replica_groups=mesh['segment'=4,'latent'=8,'tok'=4] {'tok'}, dimensions={0}, use_global_device_ids=true | all-gather | bytes 368640 | tf_op jit(solution)/shard_map/all_gather | solution.py:99
  58.0 6.4 %multiply_convert_fusion.9 = (bf16[64,2048]{1,0:T(8,128)(2,1)S(1)}, f32[64,2048]{1,0:T(8,128)}) fusion(f32[2048]{0:T(1024)S(1)} %bitcast.340, f32[2048]{0:T(1024)S(1)} %bitcast.363, bf16[64,2304]{1,0:T(8,128)(2,1)S(1)} %all_gather.34, bf16[1,2304,2048]{2,1,0:T(8,128)(2,1)} %param.11), kind=kOutput, calls=%fused_computation.77 | convolution fusion | flops 605028352 | bytes 10534912 | tf_op jit(solution)/shard_map/dot_general | solution.py:98
  99.8 6.3 %all_gather.35 = bf16[64,2304]{1,0:T(8,128)(2,1)S(1)} all-gather(bf16[16,2304]{1,0:T(8,128)(2,1)S(1)} %fusion.134), channel_id=1, replica_groups=mesh['segment'=4,'latent'=8,'tok'=4] {'tok'}, dimensions={0}, use_global_device_ids=true | all-gather | bytes 368640 | tf_op jit(solution)/shard_map/all_gather | solution.py:99
  106.1 6.5 %multiply_convert_fusion.8 = (bf16[64,2048]{1,0:T(8,128)(2,1)S(1)}, f32[64,2048]{1,0:T(8,128)}) fusion(f32[2048]{0:T(1024)S(1)} %bitcast.341, f32[2048]{0:T(1024)S(1)} %bitcast.364, bf16[64,2304]{1,0:T(8,128)(2,1)S(1)} %all_gather.35, bf16[1,2304,2048]{2,1,0:T(8,128)(2,1)} %param.11), kind=kOutput, calls=%fused_computation.75 | convolution fusion | flops 605028352 | bytes 10534912 | tf_op jit(solution)/shard_map/dot_general | solution.py:98
  148.9 5.9 %all_gather.36 = bf16[64,2304]{1,0:T(8,128)(2,1)S(1)} all-gather(bf16[16,2304]{1,0:T(8,128)(2,1)S(1)} %fusion.138), channel_id=1, replica_groups=mesh['segment'=4,'latent'=8,'tok'=4] {'tok'}, dimensions={0}, use_global_device_ids=true | all-gather | bytes 368640 | tf_op jit(solution)/shard_map/all_gather | solution.py:99
  154.8 6.5 %multiply_convert_fusion.7 = (bf16[64,2048]{1,0:T(8,128)(2,1)S(1)}, f32[64,2048]{1,0:T(8,128)}) fusion(f32[2048]{0:T(1024)S(1)} %bitcast.342, f32[2048]{0:T(1024)S(1)} %bitcast.365, bf16[64,2304]{1,0:T(8,128)(2,1)S(1)} %all_gather.36, bf16[1,2304,2048]{2,1,0:T(8,128)(2,1)} %param.11), kind=kOutput, calls=%fused_computation.73 | convolution fusion | flops 605028352 | bytes 10534912 | tf_op jit(solution)/shard_map/dot_general | solution.py:98
  166.3 4.7 collective-permute-done.19
  183.1 4.9 collective-permute-start.22
  197.9 5.9 %all_gather.37 = bf16[64,2304]{1,0:T(8,128)(2,1)S(1)} all-gather(bf16[16,2304]{1,0:T(8,128)(2,1)S(1)} %fusion.142), channel_id=1, replica_groups=mesh['segment'=4,'latent'=8,'tok'=4] {'tok'}, dimensions={0}, use_global_device_ids=true | all-gather | bytes 368640 | tf_op jit(solution)/shard_map/all_gather | solution.py:99
  203.8 6.5 %multiply_convert_fusion.6 = (bf16[64,2048]{1,0:T(8,128)(2,1)S(1)}, f32[64,2048]{1,0:T(8,128)}) fusion(f32[2048]{0:T(1024)S(1)} %bitcast.343, f32[2048]{0:T(1024)S(1)} %bitcast.366, bf16[64,2304]{1,0:T(8,128)(2,1)S(1)} %all_gather.37, bf16[1,2304,2048]{2,1,0:T(8,128)(2,1)} %param.11), kind=kOutput, calls=%fused_computation.71 | convolution fusion | flops 605028352 | bytes 10534912 | tf_op jit(solution)/shard_map/dot_general | solution.py:98
  215.4 4.7 collective-permute-done.25
  232.2 4.9 collective-permute-start.28
  247.9 5.9 %all_gather.38 = bf16[64,2304]{1,0:T(8,128)(2,1)S(1)} all-gather(bf16[16,2304]{1,0:T(8,128)(2,1)S(1)} %fusion.146), channel_id=1, replica_groups=mesh['segment'=4,'latent'=8,'tok'=4] {'tok'}, dimensions={0}, use_global_device_ids=true | all-gather | bytes 368640 | tf_op jit(solution)/shard_map/all_gather | solution.py:99
  253.8 6.5 %multiply_convert_fusion.5 = (bf16[64,2048]{1,0:T(8,128)(2,1)S(1)}, f32[64,2048]{1,0:T(8,128)}) fusion(f32[2048]{0:T(1024)S(1)} %bitcast.344, f32[2048]{0:T(1024)S(1)} %bitcast.367, bf16[64,2304]{1,0:T(8,128)(2,1)S(1)} %all_gather.38, bf16[1,2304,2048]{2,1,0:T(8,128)(2,1)} %param.11), kind=kOutput, calls=%fused_computation.69 | convolution fusion | flops 605028352 | bytes 10534912 | tf_op jit(solution)/shard_map/dot_general | solution.py:98
  265.3 4.7 collective-permute-done.31
  282.1 4.9 collective-permute-start.34
  297.8 5.9 %all_gather.39 = bf16[64,2304]{1,0:T(8,128)(2,1)S(1)} all-gather(bf16[16,2304]{1,0:T(8,128)(2,1)S(1)} %fusion.150), channel_id=1, replica_groups=mesh['segment'=4,'latent'=8,'tok'=4] {'tok'}, dimensions={0}, use_global_device_ids=true | all-gather | bytes 368640 | tf_op jit(solution)/shard_map/all_gather | solution.py:99
  303.7 6.5 %multiply_convert_fusion.4 = (bf16[64,2048]{1,0:T(8,128)(2,1)S(1)}, f32[64,2048]{1,0:T(8,128)}) fusion(f32[2048]{0:T(1024)S(1)} %bitcast.345, f32[2048]{0:T(1024)S(1)} %bitcast.368, bf16[64,2304]{1,0:T(8,128)(2,1)S(1)} %all_gather.39, bf16[1,2304,2048]{2,1,0:T(8,128)(2,1)} %param.11), kind=kOutput, calls=%fused_computation.67 | convolution fusion | flops 605028352 | bytes 10534912 | tf_op jit(solution)/shard_map/dot_general | solution.py:98
  315.1 4.7 collective-permute-done.37
  332.0 4.9 collective-permute-start.40
  347.7 6.1 %all_gather.40 = bf16[64,2304]{1,0:T(8,128)(2,1)S(1)} all-gather(bf16[16,2304]{1,0:T(8,128)(2,1)S(1)} %fusion.154), channel_id=1, replica_groups=mesh['segment'=4,'latent'=8,'tok'=4] {'tok'}, dimensions={0}, use_global_device_ids=true | all-gather | bytes 368640 | tf_op jit(solution)/shard_map/all_gather | solution.py:99
  353.8 6.5 %multiply_convert_fusion.3 = (bf16[64,2048]{1,0:T(8,128)(2,1)S(1)}, f32[64,2048]{1,0:T(8,128)}) fusion(f32[2048]{0:T(1024)S(1)} %bitcast.346, f32[2048]{0:T(1024)S(1)} %bitcast.369, bf16[64,2304]{1,0:T(8,128)(2,1)S(1)} %all_gather.40, bf16[1,2304,2048]{2,1,0:T(8,128)(2,1)} %param.11), kind=kOutput, calls=%fused_computation.65 | convolution fusion | flops 605028352 | bytes 10534912 | tf_op jit(solution)/shard_map/dot_general | solution.py:98
  387.1 5.0 collective-permute-start.46
  401.8 5.9 %all_gather.41 = bf16[64,2304]{1,0:T(8,128)(2,1)S(1)} all-gather(bf16[16,2304]{1,0:T(8,128)(2,1)S(1)} %fusion.158), channel_id=1, replica_groups=mesh['segment'=4,'latent'=8,'tok'=4] {'tok'}, dimensions={0}, use_global_device_ids=true | all-gather | bytes 368640 | tf_op jit(solution)/shard_map/all_gather | solution.py:99
  407.7 5.7 %multiply_convert_fusion.2 = (bf16[64,2048]{1,0:T(8,128)(2,1)S(1)}, f32[64,2048]{1,0:T(8,128)S(1)}) fusion(f32[2048]{0:T(1024)S(1)} %bitcast.350, f32[2048]{0:T(1024)S(1)} %bitcast.370, bf16[64,2304]{1,0:T(8,128)(2,1)S(1)} %all_gather.41, bf16[1,2304,2048]{2,1,0:T(8,128)(2,1)} %param.11), kind=kOutput, calls=%fused_computation.63 | convolution fusion | flops 605028352 | bytes 10534912 | tf_op jit(solution)/shard_map/dot_general | solution.py:98
  435.3 4.9 collective-permute-start.52
  450.1 5.9 %all_gather.42 = bf16[64,2304]{1,0:T(8,128)(2,1)S(1)} all-gather(bf16[16,2304]{1,0:T(8,128)(2,1)S(1)} %fusion.162), channel_id=1, replica_groups=mesh['segment'=4,'latent'=8,'tok'=4] {'tok'}, dimensions={0}, use_global_device_ids=true | all-gather | bytes 368640 | tf_op jit(solution)/shard_map/all_gather | solution.py:99
  479.6 4.9 collective-permute-start.58
  494.2 5.9 %all_gather.43 = bf16[64,2304]{1,0:T(8,128)(2,1)S(1)} all-gather(bf16[16,2304]{1,0:T(8,128)(2,1)S(1)} %fusion.166), channel_id=1, replica_groups=mesh['segment'=4,'latent'=8,'tok'=4] {'tok'}, dimensions={0}, use_global_device_ids=true | all-gather | bytes 368640 | tf_op jit(solution)/shard_map/all_gather | solution.py:99
  523.7 4.9 collective-permute-start.64
  (400 shorter events, 350.2 us)
Async XLA Ops:
  26.4 6.8 %collective-permute-start.2 = (f32[16,2304]{1,0:T(8,128)S(1)}, f32[16,2304]{1,0:T(8,128)S(1)}, u32[]{:S(2)}, u32[]{:S(2)}) collective-permute-start(f32[16,2304]{1,0:T(8,128)S(1)} %bitcast_add_fusion.21), channel_id=1, source_target_pairs={{0,16},{4,20},{8,24},{12,28},{16,0},{20,4},{24,8},{28,12},{1,17},{... | collective-permute-start | bytes 442376 | tf_op jit(solution)/shard_map/ppermute | solution.py:24
  38.5 6.7 %collective-permute-start.4 = (f32[16,2304]{1,0:T(8,128)S(1)}, f32[16,2304]{1,0:T(8,128)S(1)}, u32[]{:S(2)}, u32[]{:S(2)}) collective-permute-start(f32[16,2304]{1,0:T(8,128)S(1)} %add.672), channel_id=1, source_target_pairs={{0,8},{4,12},{8,0},{12,4},{16,24},{20,28},{24,16},{28,20},{1,9},{5... | collective-permute-start | bytes 442376 | tf_op jit(solution)/shard_map/ppermute | solution.py:24
  45.3 6.5 %collective-permute-start.5 = (bf16[16,2304]{1,0:T(8,128)(2,1)S(1)}, bf16[16,2304]{1,0:T(8,128)(2,1)S(1)}, u32[]{:S(2)}, u32[]{:S(2)}) collective-permute-start(bf16[16,2304]{1,0:T(8,128)(2,1)S(1)} %get-tuple-element.50), channel_id=1, source_target_pairs={{0,32},{32,64},{64,96},{1,33},{33,65},{65,97},{2,34},{34,66},{66,9... | collective-permute-start | bytes 221192 | tf_op jit(solution)/shard_map/ppermute | solution.py:19
  74.1 6.8 %collective-permute-start.8 = (f32[16,2304]{1,0:T(8,128)S(1)}, f32[16,2304]{1,0:T(8,128)S(1)}, u32[]{:S(2)}, u32[]{:S(2)}) collective-permute-start(f32[16,2304]{1,0:T(8,128)S(1)} %bitcast_add_fusion.20), channel_id=1, source_target_pairs={{0,16},{4,20},{8,24},{12,28},{16,0},{20,4},{24,8},{28,12},{1,17},{... | collective-permute-start | bytes 442376 | tf_op jit(solution)/shard_map/ppermute | solution.py:24
  86.2 6.7 %collective-permute-start.10 = (f32[16,2304]{1,0:T(8,128)S(1)}, f32[16,2304]{1,0:T(8,128)S(1)}, u32[]{:S(2)}, u32[]{:S(2)}) collective-permute-start(f32[16,2304]{1,0:T(8,128)S(1)} %add.685), channel_id=1, source_target_pairs={{0,8},{4,12},{8,0},{12,4},{16,24},{20,28},{24,16},{28,20},{1,9},{5... | collective-permute-start | bytes 442376 | tf_op jit(solution)/shard_map/ppermute | solution.py:24
  93.0 6.5 %collective-permute-start.11 = (bf16[16,2304]{1,0:T(8,128)(2,1)S(1)}, bf16[16,2304]{1,0:T(8,128)(2,1)S(1)}, u32[]{:S(2)}, u32[]{:S(2)}) collective-permute-start(bf16[16,2304]{1,0:T(8,128)(2,1)S(1)} %get-tuple-element.46), channel_id=1, source_target_pairs={{0,32},{32,64},{64,96},{1,33},{33,65},{65,97},{2,34},{34,66},{66,9... | collective-permute-start | bytes 221192 | tf_op jit(solution)/shard_map/ppermute | solution.py:19
  122.3 6.8 %collective-permute-start.14 = (f32[16,2304]{1,0:T(8,128)S(1)}, f32[16,2304]{1,0:T(8,128)S(1)}, u32[]{:S(2)}, u32[]{:S(2)}) collective-permute-start(f32[16,2304]{1,0:T(8,128)S(1)} %bitcast_add_fusion.19), channel_id=1, source_target_pairs={{0,16},{4,20},{8,24},{12,28},{16,0},{20,4},{24,8},{28,12},{1,17},{... | collective-permute-start | bytes 442376 | tf_op jit(solution)/shard_map/ppermute | solution.py:24
  134.4 7.8 %collective-permute-start.16 = (f32[16,2304]{1,0:T(8,128)S(1)}, f32[16,2304]{1,0:T(8,128)S(1)}, u32[]{:S(2)}, u32[]{:S(2)}) collective-permute-start(f32[16,2304]{1,0:T(8,128)S(1)} %add.696), channel_id=1, source_target_pairs={{0,8},{4,12},{8,0},{12,4},{16,24},{20,28},{24,16},{28,20},{1,9},{5... | collective-permute-start | bytes 442376 | tf_op jit(solution)/shard_map/ppermute | solution.py:24
  142.2 6.5 %collective-permute-start.17 = (bf16[16,2304]{1,0:T(8,128)(2,1)S(1)}, bf16[16,2304]{1,0:T(8,128)(2,1)S(1)}, u32[]{:S(2)}, u32[]{:S(2)}) collective-permute-start(bf16[16,2304]{1,0:T(8,128)(2,1)S(1)} %get-tuple-element.42), channel_id=1, source_target_pairs={{0,32},{32,64},{64,96},{1,33},{33,65},{65,97},{2,34},{34,66},{66,9... | collective-permute-start | bytes 221192 | tf_op jit(solution)/shard_map/ppermute | solution.py:19
  171.0 6.8 %collective-permute-start.20 = (f32[16,2304]{1,0:T(8,128)S(1)}, f32[16,2304]{1,0:T(8,128)S(1)}, u32[]{:S(2)}, u32[]{:S(2)}) collective-permute-start(f32[16,2304]{1,0:T(8,128)S(1)} %bitcast_add_fusion.18), channel_id=1, source_target_pairs={{0,16},{4,20},{8,24},{12,28},{16,0},{20,4},{24,8},{28,12},{1,17},{... | collective-permute-start | bytes 442376 | tf_op jit(solution)/shard_map/ppermute | solution.py:24
  183.1 8.0 %collective-permute-start.22 = (f32[16,2304]{1,0:T(8,128)S(1)}, f32[16,2304]{1,0:T(8,128)S(1)}, u32[]{:S(2)}, u32[]{:S(2)}) collective-permute-start(f32[16,2304]{1,0:T(8,128)S(1)} %add.707), channel_id=1, source_target_pairs={{0,8},{4,12},{8,0},{12,4},{16,24},{20,28},{24,16},{28,20},{1,9},{5... | collective-permute-start | bytes 442376 | tf_op jit(solution)/shard_map/ppermute | solution.py:24
  191.2 6.5 %collective-permute-start.23 = (bf16[16,2304]{1,0:T(8,128)(2,1)S(1)}, bf16[16,2304]{1,0:T(8,128)(2,1)S(1)}, u32[]{:S(2)}, u32[]{:S(2)}) collective-permute-start(bf16[16,2304]{1,0:T(8,128)(2,1)S(1)} %get-tuple-element.38), channel_id=1, source_target_pairs={{0,32},{32,64},{64,96},{1,33},{33,65},{65,97},{2,34},{34,66},{66,9... | collective-permute-start | bytes 221192 | tf_op jit(solution)/shard_map/ppermute | solution.py:19
  220.2 6.8 %collective-permute-start.26 = (f32[16,2304]{1,0:T(8,128)S(1)}, f32[16,2304]{1,0:T(8,128)S(1)}, u32[]{:S(2)}, u32[]{:S(2)}) collective-permute-start(f32[16,2304]{1,0:T(8,128)S(1)} %bitcast_add_fusion.17), channel_id=1, source_target_pairs={{0,16},{4,20},{8,24},{12,28},{16,0},{20,4},{24,8},{28,12},{1,17},{... | collective-permute-start | bytes 442376 | tf_op jit(solution)/shard_map/ppermute | solution.py:24
  232.2 8.0 %collective-permute-start.28 = (f32[16,2304]{1,0:T(8,128)S(1)}, f32[16,2304]{1,0:T(8,128)S(1)}, u32[]{:S(2)}, u32[]{:S(2)}) collective-permute-start(f32[16,2304]{1,0:T(8,128)S(1)} %add.718), channel_id=1, source_target_pairs={{0,8},{4,12},{8,0},{12,4},{16,24},{20,28},{24,16},{28,20},{1,9},{5... | collective-permute-start | bytes 442376 | tf_op jit(solution)/shard_map/ppermute | solution.py:24
  240.3 6.5 %collective-permute-start.29 = (bf16[16,2304]{1,0:T(8,128)(2,1)S(1)}, bf16[16,2304]{1,0:T(8,128)(2,1)S(1)}, u32[]{:S(2)}, u32[]{:S(2)}) collective-permute-start(bf16[16,2304]{1,0:T(8,128)(2,1)S(1)} %get-tuple-element.34), channel_id=1, source_target_pairs={{0,32},{32,64},{64,96},{1,33},{33,65},{65,97},{2,34},{34,66},{66,9... | collective-permute-start | bytes 221192 | tf_op jit(solution)/shard_map/ppermute | solution.py:19
  270.0 6.8 %collective-permute-start.32 = (f32[16,2304]{1,0:T(8,128)S(1)}, f32[16,2304]{1,0:T(8,128)S(1)}, u32[]{:S(2)}, u32[]{:S(2)}) collective-permute-start(f32[16,2304]{1,0:T(8,128)S(1)} %bitcast_add_fusion.16), channel_id=1, source_target_pairs={{0,16},{4,20},{8,24},{12,28},{16,0},{20,4},{24,8},{28,12},{1,17},{... | collective-permute-start | bytes 442376 | tf_op jit(solution)/shard_map/ppermute | solution.py:24
  282.1 8.0 %collective-permute-start.34 = (f32[16,2304]{1,0:T(8,128)S(1)}, f32[16,2304]{1,0:T(8,128)S(1)}, u32[]{:S(2)}, u32[]{:S(2)}) collective-permute-start(f32[16,2304]{1,0:T(8,128)S(1)} %add.729), channel_id=1, source_target_pairs={{0,8},{4,12},{8,0},{12,4},{16,24},{20,28},{24,16},{28,20},{1,9},{5... | collective-permute-start | bytes 442376 | tf_op jit(solution)/shard_map/ppermute | solution.py:24
  290.2 6.5 %collective-permute-start.35 = (bf16[16,2304]{1,0:T(8,128)(2,1)S(1)}, bf16[16,2304]{1,0:T(8,128)(2,1)S(1)}, u32[]{:S(2)}, u32[]{:S(2)}) collective-permute-start(bf16[16,2304]{1,0:T(8,128)(2,1)S(1)} %get-tuple-element.30), channel_id=1, source_target_pairs={{0,32},{32,64},{64,96},{1,33},{33,65},{65,97},{2,34},{34,66},{66,9... | collective-permute-start | bytes 221192 | tf_op jit(solution)/shard_map/ppermute | solution.py:19
  319.9 6.8 %collective-permute-start.38 = (f32[16,2304]{1,0:T(8,128)S(1)}, f32[16,2304]{1,0:T(8,128)S(1)}, u32[]{:S(2)}, u32[]{:S(2)}) collective-permute-start(f32[16,2304]{1,0:T(8,128)S(1)} %bitcast_add_fusion.15), channel_id=1, source_target_pairs={{0,16},{4,20},{8,24},{12,28},{16,0},{20,4},{24,8},{28,12},{1,17},{... | collective-permute-start | bytes 442376 | tf_op jit(solution)/shard_map/ppermute | solution.py:24
  332.0 8.0 %collective-permute-start.40 = (f32[16,2304]{1,0:T(8,128)S(1)}, f32[16,2304]{1,0:T(8,128)S(1)}, u32[]{:S(2)}, u32[]{:S(2)}) collective-permute-start(f32[16,2304]{1,0:T(8,128)S(1)} %add.740), channel_id=1, source_target_pairs={{0,8},{4,12},{8,0},{12,4},{16,24},{20,28},{24,16},{28,20},{1,9},{5... | collective-permute-start | bytes 442376 | tf_op jit(solution)/shard_map/ppermute | solution.py:24
  340.0 6.5 %collective-permute-start.41 = (bf16[16,2304]{1,0:T(8,128)(2,1)S(1)}, bf16[16,2304]{1,0:T(8,128)(2,1)S(1)}, u32[]{:S(2)}, u32[]{:S(2)}) collective-permute-start(bf16[16,2304]{1,0:T(8,128)(2,1)S(1)} %get-tuple-element.26), channel_id=1, source_target_pairs={{0,32},{32,64},{64,96},{1,33},{33,65},{65,97},{2,34},{34,66},{66,9... | collective-permute-start | bytes 221192 | tf_op jit(solution)/shard_map/ppermute | solution.py:19
  375.1 6.7 %collective-permute-start.44 = (f32[16,2304]{1,0:T(8,128)S(1)}, f32[16,2304]{1,0:T(8,128)S(1)}, u32[]{:S(2)}, u32[]{:S(2)}) collective-permute-start(f32[16,2304]{1,0:T(8,128)S(1)} %bitcast_add_fusion.14), channel_id=1, source_target_pairs={{0,16},{4,20},{8,24},{12,28},{16,0},{20,4},{24,8},{28,12},{1,17},{... | collective-permute-start | bytes 442376 | tf_op jit(solution)/shard_map/ppermute | solution.py:24
  387.1 8.1 %collective-permute-start.46 = (f32[16,2304]{1,0:T(8,128)S(1)}, f32[16,2304]{1,0:T(8,128)S(1)}, u32[]{:S(2)}, u32[]{:S(2)}) collective-permute-start(f32[16,2304]{1,0:T(8,128)S(1)} %add.751), channel_id=1, source_target_pairs={{0,8},{4,12},{8,0},{12,4},{16,24},{20,28},{24,16},{28,20},{1,9},{5... | collective-permute-start | bytes 442376 | tf_op jit(solution)/shard_map/ppermute | solution.py:24
  395.3 6.2 %collective-permute-start.47 = (bf16[16,2304]{1,0:T(8,128)(2,1)S(1)}, bf16[16,2304]{1,0:T(8,128)(2,1)S(1)}, u32[]{:S(2)}, u32[]{:S(2)}) collective-permute-start(bf16[16,2304]{1,0:T(8,128)(2,1)S(1)} %get-tuple-element.22), channel_id=1, source_target_pairs={{0,32},{32,64},{64,96},{1,33},{33,65},{65,97},{2,34},{34,66},{66,9... | collective-permute-start | bytes 221192 | tf_op jit(solution)/shard_map/ppermute | solution.py:19
  423.2 6.8 %collective-permute-start.50 = (f32[16,2304]{1,0:T(8,128)S(1)}, f32[16,2304]{1,0:T(8,128)S(1)}, u32[]{:S(2)}, u32[]{:S(2)}) collective-permute-start(f32[16,2304]{1,0:T(8,128)S(1)} %bitcast_add_fusion.13), channel_id=1, source_target_pairs={{0,16},{4,20},{8,24},{12,28},{16,0},{20,4},{24,8},{28,12},{1,17},{... | collective-permute-start | bytes 442376 | tf_op jit(solution)/shard_map/ppermute | solution.py:24
  435.3 8.0 %collective-permute-start.52 = (f32[16,2304]{1,0:T(8,128)S(1)}, f32[16,2304]{1,0:T(8,128)S(1)}, u32[]{:S(2)}, u32[]{:S(2)}) collective-permute-start(f32[16,2304]{1,0:T(8,128)S(1)} %add.762), channel_id=1, source_target_pairs={{0,8},{4,12},{8,0},{12,4},{16,24},{20,28},{24,16},{28,20},{1,9},{5... | collective-permute-start | bytes 442376 | tf_op jit(solution)/shard_map/ppermute | solution.py:24
  443.3 6.5 %collective-permute-start.53 = (bf16[16,2304]{1,0:T(8,128)(2,1)S(1)}, bf16[16,2304]{1,0:T(8,128)(2,1)S(1)}, u32[]{:S(2)}, u32[]{:S(2)}) collective-permute-start(bf16[16,2304]{1,0:T(8,128)(2,1)S(1)} %get-tuple-element.20), channel_id=1, source_target_pairs={{0,32},{32,64},{64,96},{1,33},{33,65},{65,97},{2,34},{34,66},{66,9... | collective-permute-start | bytes 221192 | tf_op jit(solution)/shard_map/ppermute | solution.py:19
  467.5 6.8 %collective-permute-start.56 = (f32[16,2304]{1,0:T(8,128)S(1)}, f32[16,2304]{1,0:T(8,128)S(1)}, u32[]{:S(2)}, u32[]{:S(2)}) collective-permute-start(f32[16,2304]{1,0:T(8,128)S(1)} %bitcast_add_fusion.12), channel_id=1, source_target_pairs={{0,16},{4,20},{8,24},{12,28},{16,0},{20,4},{24,8},{28,12},{1,17},{... | collective-permute-start | bytes 442376 | tf_op jit(solution)/shard_map/ppermute | solution.py:24
  479.6 8.0 %collective-permute-start.58 = (f32[16,2304]{1,0:T(8,128)S(1)}, f32[16,2304]{1,0:T(8,128)S(1)}, u32[]{:S(2)}, u32[]{:S(2)}) collective-permute-start(f32[16,2304]{1,0:T(8,128)S(1)} %add.773), channel_id=1, source_target_pairs={{0,8},{4,12},{8,0},{12,4},{16,24},{20,28},{24,16},{28,20},{1,9},{5... | collective-permute-start | bytes 442376 | tf_op jit(solution)/shard_map/ppermute | solution.py:24
  487.7 6.2 %collective-permute-start.59 = (bf16[16,2304]{1,0:T(8,128)(2,1)S(1)}, bf16[16,2304]{1,0:T(8,128)(2,1)S(1)}, u32[]{:S(2)}, u32[]{:S(2)}) collective-permute-start(bf16[16,2304]{1,0:T(8,128)(2,1)S(1)} %get-tuple-element.18), channel_id=1, source_target_pairs={{0,32},{32,64},{64,96},{1,33},{33,65},{65,97},{2,34},{34,66},{66,9... | collective-permute-start | bytes 221192 | tf_op jit(solution)/shard_map/ppermute | solution.py:19
  511.6 6.8 %collective-permute-start.62 = (f32[16,2304]{1,0:T(8,128)S(1)}, f32[16,2304]{1,0:T(8,128)S(1)}, u32[]{:S(2)}, u32[]{:S(2)}) collective-permute-start(f32[16,2304]{1,0:T(8,128)S(1)} %bitcast_add_fusion.11), channel_id=1, source_target_pairs={{0,16},{4,20},{8,24},{12,28},{16,0},{20,4},{24,8},{28,12},{1,17},{... | collective-permute-start | bytes 442376 | tf_op jit(solution)/shard_map/ppermute | solution.py:24
  523.7 8.0 %collective-permute-start.64 = (f32[16,2304]{1,0:T(8,128)S(1)}, f32[16,2304]{1,0:T(8,128)S(1)}, u32[]{:S(2)}, u32[]{:S(2)}) collective-permute-start(f32[16,2304]{1,0:T(8,128)S(1)} %add.784), channel_id=1, source_target_pairs={{0,8},{4,12},{8,0},{12,4},{16,24},{20,28},{24,16},{28,20},{1,9},{5... | collective-permute-start | bytes 442376 | tf_op jit(solution)/shard_map/ppermute | solution.py:24
  (77 other events, 796.7 us)

commit v2 on v1

--- a/solution.py
+++ b/solution.py
@@ -4,7 +4,7 @@
 from jax.sharding import PartitionSpec as P
 
 ROWS_DEV = 128
-MICRO = 8
+MICRO = 4
 BLOCKS = 8
 
 
@@ -36,9 +36,19 @@
     keep = lax.dynamic_index_in_dim(halves, low, axis=0, keepdims=False)
     send = lax.dynamic_index_in_dim(halves, 1 - low, axis=0, keepdims=False)
     total = keep + swap_with(send, "tok", 2)
-    for bit in (4, 1, 2):
-        total = total + swap_with(total, "latent", bit)
+    for step in range(3):
+        total = total + lax.ppermute(total, ("latent", "tok"), latent_round(step))
     return total
+
+
+def latent_round(step):
+    orders = ((4, 1, 2), (2, 4, 1))
+    pairs = []
+    for latent in range(8):
+        for tok in range(4):
+            bit = orders[tok % 2][step]
+            pairs.append((latent * 4 + tok, (latent ^ bit) * 4 + tok))
+    return pairs
 
 
 def per_device(

time: 542 us -> 422 us (0.78)
  starting transfers between devices: 164 us -> 68.9 us
  matrix products: 87.4 us -> 62.6 us
  waiting for transfers between devices: 194 us -> 211 us
  blocking collectives: 65.4 us -> 50 us
    ppermute x0 -> x21, waiting for transfers between devices: none -> 126 us  [reduce_rows(): total = total + lax.ppermute(total, ('latent', 'tok'), latent_round(step))]
    ppermute x55 -> x14, starting transfers between devices: 127 us -> 11.5 us  [swap_with(): return lax.ppermute(array, axis, [(i, i ^ bit) for i in range(devices)])]
    ppermute x55 -> x14, waiting for transfers between devices: 169 us -> 64.8 us  [swap_with(): return lax.ppermute(array, axis, [(i, i ^ bit) for i in range(devices)])]
    ppermute x0 -> x21, starting transfers between devices: none -> 35.7 us  [reduce_rows(): total = total + lax.ppermute(total, ('latent', 'tok'), latent_round(step))]
    ppermute x10 -> x6, starting transfers between devices: 37.4 us -> 21.8 us  [from_behind(): return lax.ppermute(array, axis, pairs)]
    dot_general x11 -> x7, matrix products: 61.1 us -> 45.5 us  [per_device(): jnp.dot(lax.all_gather(normed, 'tok', axis=0, tiled=True), encoder, prefe...]
    all_gather x11 -> x7, blocking collectives: 65.4 us -> 50 us  [per_device(): lax.all_gather(normed, 'tok', axis=0, tiled=True)]
    dot_general x11 -> x7, matrix products: 18.9 us -> 9.96 us  [per_device(): partial_sum = jnp.dot(latents, decoder, preferred_element_type=jnp.float32)]
  transfers between devices with their start and end apart: 65 -> 41, of which waited for: 64 -> 41; matrix products, arithmetic and copies ran while one was open for 2% -> 3% of each run, Pallas kernels for 0% -> 0%
where the time goes in v2:
time: 422 us; the launch traced here: 414 us
  waiting for transfers between devices  211 us (50%)
  starting transfers between devices  68.9 us (16%)
  matrix products  62.6 us (15%)
  blocking collectives  50 us (12%)
  other arithmetic  11.6 us (3%)
  local copies, waits for them, and re-layouts  7.69 us (2%)
    ppermute x21, waiting for transfers between devices, reduce_rows(): total = total + lax.ppermute(total, ('latent', 'tok'), latent_round(step))  126 us
    ppermute x14, waiting for transfers between devices, swap_with(): return lax.ppermute(array, axis, [(i, i ^ bit) for i in range(devices)])  64.8 us
    all_gather x7, blocking collectives, per_device(): lax.all_gather(normed, 'tok', axis=0, tiled=True)  50 us
    dot_general x7, matrix products, per_device(): jnp.dot(lax.all_gather(normed, 'tok', axis=0, tiled=True), encoder, prefe...  45.5 us
    ppermute x21, starting transfers between devices, reduce_rows(): total = total + lax.ppermute(total, ('latent', 'tok'), latent_round(step))  35.7 us
    ppermute x6, starting transfers between devices, from_behind(): return lax.ppermute(array, axis, pairs)  21.8 us
    ppermute x6, waiting for transfers between devices, from_behind(): return lax.ppermute(array, axis, pairs)  20.1 us
    ppermute x14, starting transfers between devices, swap_with(): return lax.ppermute(array, axis, [(i, i ^ bit) for i in range(devices)])  11.5 us
  transfers between devices with their start and end apart: 41, of which 41 were waited for; matrix products, arithmetic and copies ran while one was open for 3% of the time, Pallas kernels for 0%

profile of v2, /device:TPU:64, one launch (start us, length us, event | category | flops | bytes accessed | tf_op | source)
XLA Modules:
  0.0 413.9 jit_solution(15976301307020376354)
XLA Ops:
  4.2 7.7 %all_gather.21 = bf16[128,2304]{1,0:T(8,128)(2,1)S(1)} all-gather(bf16[32,2304]{1,0:T(8,128)(2,1)S(1)} %fusion.82), channel_id=1, replica_groups=mesh['segment'=4,'latent'=8,'tok'=4] {'tok'}, dimensions={0}, use_global_device_ids=true | all-gather | bytes 737280 | tf_op jit(solution)/shard_map/all_gather | solution.py:109
  11.9 6.7 %broadcast_select_fusion = (bf16[128,2048]{1,0:T(8,128)(2,1)}, bf16[128,2048]{1,0:T(8,128)(2,1)S(1)}, f32[128,2048]{1,0:T(8,128)}) fusion(pred[]{:T(512)S(6)} %and.45, f32[2048]{0:T(1024)S(1)} %bitcast.255, f32[2048]{0:T(1024)} %bitcast.269, bf16[128,2304]{1,0:T(8,128)(2,1)S(1)} %all_gather.21, bf16[1,2304,2048]{2,1,0:T(8,128)(2,1)} %param.11), kind=kOutput, calls=%fused_computation.101 | convolution fusion | flops 1210318848 | bytes 12140545 | tf_op jit(solution)/shard_map/dot_general | solution.py:108
  23.5 8.2 %collective-permute-done.1 = f32[32,2304]{1,0:T(8,128)S(1)} collective-permute-done((f32[32,2304]{1,0:T(8,128)S(1)}, f32[32,2304]{1,0:T(8,128)S(1)}, u32[]{:S(2)}, u32[]{:S(2)}) %collective-permute-start.1) | collective-permute-done | bytes 294944 | tf_op jit(solution)/shard_map/ppermute | solution.py:24
  50.1 7.0 %collective-permute-done.4 = f32[32,2304]{1,0:T(8,128)S(1)} collective-permute-done((f32[32,2304]{1,0:T(8,128)S(1)}, f32[32,2304]{1,0:T(8,128)S(1)}, u32[]{:S(2)}, u32[]{:S(2)}) %collective-permute-start.4) | collective-permute-done | bytes 294944 | tf_op jit(solution)/shard_map/ppermute | solution.py:40
  64.6 7.0 %all_gather.22 = bf16[128,2304]{1,0:T(8,128)(2,1)S(1)} all-gather(bf16[32,2304]{1,0:T(8,128)(2,1)S(1)} %fusion.86), channel_id=1, replica_groups=mesh['segment'=4,'latent'=8,'tok'=4] {'tok'}, dimensions={0}, use_global_device_ids=true | all-gather | bytes 737280 | tf_op jit(solution)/shard_map/all_gather | solution.py:109
  71.5 6.5 %multiply_convert_fusion.5 = (bf16[128,2048]{1,0:T(8,128)(2,1)S(1)}, f32[128,2048]{1,0:T(8,128)}) fusion(f32[2048]{0:T(1024)S(1)} %bitcast.256, f32[2048]{0:T(1024)S(1)} %bitcast.270, bf16[128,2304]{1,0:T(8,128)(2,1)S(1)} %all_gather.22, bf16[1,2304,2048]{2,1,0:T(8,128)(2,1)} %param.11), kind=kOutput, calls=%fused_computation.49 | convolution fusion | flops 1210056704 | bytes 11616256 | tf_op jit(solution)/shard_map/dot_general | solution.py:108
  83.1 8.0 %collective-permute-done.7 = f32[32,2304]{1,0:T(8,128)S(1)} collective-permute-done((f32[32,2304]{1,0:T(8,128)S(1)}, f32[32,2304]{1,0:T(8,128)S(1)}, u32[]{:S(2)}, u32[]{:S(2)}) %collective-permute-start.7) | collective-permute-done | bytes 294944 | tf_op jit(solution)/shard_map/ppermute | solution.py:24
  100.1 6.2 %collective-permute-done.9 = f32[32,2304]{1,0:T(8,128)S(1)} collective-permute-done((f32[32,2304]{1,0:T(8,128)S(1)}, f32[32,2304]{1,0:T(8,128)S(1)}, u32[]{:S(2)}, u32[]{:S(2)}) %collective-permute-start.9) | collective-permute-done | bytes 294944 | tf_op jit(solution)/shard_map/ppermute | solution.py:40
  108.0 7.0 %collective-permute-done.10 = f32[32,2304]{1,0:T(8,128)S(1)} collective-permute-done((f32[32,2304]{1,0:T(8,128)S(1)}, f32[32,2304]{1,0:T(8,128)S(1)}, u32[]{:S(2)}, u32[]{:S(2)}) %collective-permute-start.10) | collective-permute-done | bytes 294944 | tf_op jit(solution)/shard_map/ppermute | solution.py:40
  122.4 7.3 %all_gather.23 = bf16[128,2304]{1,0:T(8,128)(2,1)S(1)} all-gather(bf16[32,2304]{1,0:T(8,128)(2,1)S(1)} %fusion.90), channel_id=1, replica_groups=mesh['segment'=4,'latent'=8,'tok'=4] {'tok'}, dimensions={0}, use_global_device_ids=true | all-gather | bytes 737280 | tf_op jit(solution)/shard_map/all_gather | solution.py:109
  129.7 6.7 %multiply_convert_fusion.4 = (bf16[128,2048]{1,0:T(8,128)(2,1)S(1)}, f32[128,2048]{1,0:T(8,128)}) fusion(f32[2048]{0:T(1024)S(1)} %bitcast.257, f32[2048]{0:T(1024)S(1)} %bitcast.271, bf16[128,2304]{1,0:T(8,128)(2,1)S(1)} %all_gather.23, bf16[1,2304,2048]{2,1,0:T(8,128)(2,1)} %param.11), kind=kOutput, calls=%fused_computation.47 | convolution fusion | flops 1210056704 | bytes 11616256 | tf_op jit(solution)/shard_map/dot_general | solution.py:108
  141.2 8.2 %collective-permute-done.13 = f32[32,2304]{1,0:T(8,128)S(1)} collective-permute-done((f32[32,2304]{1,0:T(8,128)S(1)}, f32[32,2304]{1,0:T(8,128)S(1)}, u32[]{:S(2)}, u32[]{:S(2)}) %collective-permute-start.13) | collective-permute-done | bytes 294944 | tf_op jit(solution)/shard_map/ppermute | solution.py:24
  158.1 6.5 %collective-permute-done.15 = f32[32,2304]{1,0:T(8,128)S(1)} collective-permute-done((f32[32,2304]{1,0:T(8,128)S(1)}, f32[32,2304]{1,0:T(8,128)S(1)}, u32[]{:S(2)}, u32[]{:S(2)}) %collective-permute-start.15) | collective-permute-done | bytes 294944 | tf_op jit(solution)/shard_map/ppermute | solution.py:40
  166.2 7.9 %collective-permute-done.16 = f32[32,2304]{1,0:T(8,128)S(1)} collective-permute-done((f32[32,2304]{1,0:T(8,128)S(1)}, f32[32,2304]{1,0:T(8,128)S(1)}, u32[]{:S(2)}, u32[]{:S(2)}) %collective-permute-start.16) | collective-permute-done | bytes 294944 | tf_op jit(solution)/shard_map/ppermute | solution.py:40
  181.5 7.0 %all_gather.24 = bf16[128,2304]{1,0:T(8,128)(2,1)S(1)} all-gather(bf16[32,2304]{1,0:T(8,128)(2,1)S(1)} %fusion.94), channel_id=1, replica_groups=mesh['segment'=4,'latent'=8,'tok'=4] {'tok'}, dimensions={0}, use_global_device_ids=true | all-gather | bytes 737280 | tf_op jit(solution)/shard_map/all_gather | solution.py:109
  188.5 6.6 %multiply_convert_fusion.3 = (bf16[128,2048]{1,0:T(8,128)(2,1)S(1)}, f32[128,2048]{1,0:T(8,128)}) fusion(f32[2048]{0:T(1024)S(1)} %bitcast.258, f32[2048]{0:T(1024)S(1)} %bitcast.272, bf16[128,2304]{1,0:T(8,128)(2,1)S(1)} %all_gather.24, bf16[1,2304,2048]{2,1,0:T(8,128)(2,1)} %param.11), kind=kOutput, calls=%fused_computation.45 | convolution fusion | flops 1210056704 | bytes 11616256 | tf_op jit(solution)/shard_map/dot_general | solution.py:108
  200.2 8.1 %collective-permute-done.19 = f32[32,2304]{1,0:T(8,128)S(1)} collective-permute-done((f32[32,2304]{1,0:T(8,128)S(1)}, f32[32,2304]{1,0:T(8,128)S(1)}, u32[]{:S(2)}, u32[]{:S(2)}) %collective-permute-start.19) | collective-permute-done | bytes 294944 | tf_op jit(solution)/shard_map/ppermute | solution.py:24
  216.7 6.7 %collective-permute-done.21 = f32[32,2304]{1,0:T(8,128)S(1)} collective-permute-done((f32[32,2304]{1,0:T(8,128)S(1)}, f32[32,2304]{1,0:T(8,128)S(1)}, u32[]{:S(2)}, u32[]{:S(2)}) %collective-permute-start.21) | collective-permute-done | bytes 294944 | tf_op jit(solution)/shard_map/ppermute | solution.py:40
  224.2 7.9 %collective-permute-done.22 = f32[32,2304]{1,0:T(8,128)S(1)} collective-permute-done((f32[32,2304]{1,0:T(8,128)S(1)}, f32[32,2304]{1,0:T(8,128)S(1)}, u32[]{:S(2)}, u32[]{:S(2)}) %collective-permute-start.22) | collective-permute-done | bytes 294944 | tf_op jit(solution)/shard_map/ppermute | solution.py:40
  239.7 7.2 %all_gather.25 = bf16[128,2304]{1,0:T(8,128)(2,1)S(1)} all-gather(bf16[32,2304]{1,0:T(8,128)(2,1)S(1)} %fusion.98), channel_id=1, replica_groups=mesh['segment'=4,'latent'=8,'tok'=4] {'tok'}, dimensions={0}, use_global_device_ids=true | all-gather | bytes 737280 | tf_op jit(solution)/shard_map/all_gather | solution.py:109
  246.9 6.6 %multiply_convert_fusion.2 = (bf16[128,2048]{1,0:T(8,128)(2,1)S(1)}, f32[128,2048]{1,0:T(8,128)}) fusion(f32[2048]{0:T(1024)S(1)} %bitcast.259, f32[2048]{0:T(1024)S(1)} %bitcast.273, bf16[128,2304]{1,0:T(8,128)(2,1)S(1)} %all_gather.25, bf16[1,2304,2048]{2,1,0:T(8,128)(2,1)} %param.11), kind=kOutput, calls=%fused_computation.43 | convolution fusion | flops 1210056704 | bytes 11616256 | tf_op jit(solution)/shard_map/dot_general | solution.py:108
  258.4 8.2 %collective-permute-done.25 = f32[32,2304]{1,0:T(8,128)S(1)} collective-permute-done((f32[32,2304]{1,0:T(8,128)S(1)}, f32[32,2304]{1,0:T(8,128)S(1)}, u32[]{:S(2)}, u32[]{:S(2)}) %collective-permute-start.25) | collective-permute-done | bytes 294944 | tf_op jit(solution)/shard_map/ppermute | solution.py:24
  275.1 6.7 %collective-permute-done.27 = f32[32,2304]{1,0:T(8,128)S(1)} collective-permute-done((f32[32,2304]{1,0:T(8,128)S(1)}, f32[32,2304]{1,0:T(8,128)S(1)}, u32[]{:S(2)}, u32[]{:S(2)}) %collective-permute-start.27) | collective-permute-done | bytes 294944 | tf_op jit(solution)/shard_map/ppermute | solution.py:40
  283.4 7.9 %collective-permute-done.28 = f32[32,2304]{1,0:T(8,128)S(1)} collective-permute-done((f32[32,2304]{1,0:T(8,128)S(1)}, f32[32,2304]{1,0:T(8,128)S(1)}, u32[]{:S(2)}, u32[]{:S(2)}) %collective-permute-start.28) | collective-permute-done | bytes 294944 | tf_op jit(solution)/shard_map/ppermute | solution.py:40
  299.0 6.8 %all_gather.26 = bf16[128,2304]{1,0:T(8,128)(2,1)S(1)} all-gather(bf16[32,2304]{1,0:T(8,128)(2,1)S(1)} %fusion.102), channel_id=1, replica_groups=mesh['segment'=4,'latent'=8,'tok'=4] {'tok'}, dimensions={0}, use_global_device_ids=true | all-gather | bytes 737280 | tf_op jit(solution)/shard_map/all_gather | solution.py:109
  305.9 6.7 %multiply_convert_fusion.1 = (bf16[128,2048]{1,0:T(8,128)(2,1)S(1)}, f32[128,2048]{1,0:T(8,128)}) fusion(f32[2048]{0:T(1024)S(1)} %bitcast.260, f32[2048]{0:T(1024)S(1)} %bitcast.274, bf16[128,2304]{1,0:T(8,128)(2,1)S(1)} %all_gather.26, bf16[1,2304,2048]{2,1,0:T(8,128)(2,1)} %param.11), kind=kOutput, calls=%fused_computation.41 | convolution fusion | flops 1210056704 | bytes 11616256 | tf_op jit(solution)/shard_map/dot_general | solution.py:108
  320.8 6.6 %collective-permute-done.31 = f32[32,2304]{1,0:T(8,128)} collective-permute-done((f32[32,2304]{1,0:T(8,128)}, f32[32,2304]{1,0:T(8,128)}, u32[]{:S(2)}, u32[]{:S(2)}) %collective-permute-start.31) | collective-permute-done | bytes 294944 | tf_op jit(solution)/shard_map/ppermute | solution.py:24
  339.9 5.7 %collective-permute-done.33 = f32[32,2304]{1,0:T(8,128)S(1)} collective-permute-done((f32[32,2304]{1,0:T(8,128)S(1)}, f32[32,2304]{1,0:T(8,128)S(1)}, u32[]{:S(2)}, u32[]{:S(2)}) %collective-permute-start.33) | collective-permute-done | bytes 294944 | tf_op jit(solution)/shard_map/ppermute | solution.py:40
  346.7 7.7 %collective-permute-done.34 = f32[32,2304]{1,0:T(8,128)S(1)} collective-permute-done((f32[32,2304]{1,0:T(8,128)S(1)}, f32[32,2304]{1,0:T(8,128)S(1)}, u32[]{:S(2)}, u32[]{:S(2)}) %collective-permute-start.34) | collective-permute-done | bytes 294944 | tf_op jit(solution)/shard_map/ppermute | solution.py:40
  361.9 7.0 %all_gather.27 = bf16[128,2304]{1,0:T(8,128)(2,1)S(1)} all-gather(bf16[32,2304]{1,0:T(8,128)(2,1)S(1)} %fusion.106), channel_id=1, replica_groups=mesh['segment'=4,'latent'=8,'tok'=4] {'tok'}, dimensions={0}, use_global_device_ids=true | all-gather | bytes 737280 | tf_op jit(solution)/shard_map/all_gather | solution.py:109
  380.4 7.2 %collective-permute-done.37 = f32[32,2304]{1,0:T(8,128)S(1)} collective-permute-done((f32[32,2304]{1,0:T(8,128)S(1)}, f32[32,2304]{1,0:T(8,128)S(1)}, u32[]{:S(2)}, u32[]{:S(2)}) %collective-permute-start.37) | collective-permute-done | bytes 294944 | tf_op jit(solution)/shard_map/ppermute | solution.py:24
  396.3 6.5 %collective-permute-done.39 = f32[32,2304]{1,0:T(8,128)S(1)} collective-permute-done((f32[32,2304]{1,0:T(8,128)S(1)}, f32[32,2304]{1,0:T(8,128)S(1)}, u32[]{:S(2)}, u32[]{:S(2)}) %collective-permute-start.39) | collective-permute-done | bytes 294944 | tf_op jit(solution)/shard_map/ppermute | solution.py:40
  (283 shorter events, 183.8 us)
Async XLA Ops:
  22.3 9.3 %collective-permute-start.1 = (f32[32,2304]{1,0:T(8,128)S(1)}, f32[32,2304]{1,0:T(8,128)S(1)}, u32[]{:S(2)}, u32[]{:S(2)}) collective-permute-start(f32[32,2304]{1,0:T(8,128)S(1)} %dynamic-slice_bitcast_fusion.13), channel_id=1, source_target_pairs={{0,2},{1,3},{2,0},{3,1},{4,6},{5,7},{6,4},{7,5},{8,10},{9,11},{10,... | collective-permute-start | bytes 884744 | tf_op jit(solution)/shard_map/ppermute | solution.py:24
  31.7 8.3 %collective-permute-start.2 = (f32[32,2304]{1,0:T(8,128)S(1)}, f32[32,2304]{1,0:T(8,128)S(1)}, u32[]{:S(2)}, u32[]{:S(2)}) collective-permute-start(f32[32,2304]{1,0:T(8,128)S(1)} %bitcast_add_fusion.13), channel_id=1, source_target_pairs={{0,16},{1,9},{2,18},{3,11},{4,20},{5,13},{6,22},{7,15},{8,24},{9,1... | collective-permute-start | bytes 884744 | tf_op jit(solution)/shard_map/ppermute | solution.py:40
  40.1 6.8 %collective-permute-start.3 = (f32[32,2304]{1,0:T(8,128)S(1)}, f32[32,2304]{1,0:T(8,128)S(1)}, u32[]{:S(2)}, u32[]{:S(2)}) collective-permute-start(f32[32,2304]{1,0:T(8,128)S(1)} %add.439), channel_id=1, source_target_pairs={{0,4},{1,17},{2,6},{3,19},{4,0},{5,21},{6,2},{7,23},{8,12},{9,25},... | collective-permute-start | bytes 884744 | tf_op jit(solution)/shard_map/ppermute | solution.py:40
  46.9 10.2 %collective-permute-start.4 = (f32[32,2304]{1,0:T(8,128)S(1)}, f32[32,2304]{1,0:T(8,128)S(1)}, u32[]{:S(2)}, u32[]{:S(2)}) collective-permute-start(f32[32,2304]{1,0:T(8,128)S(1)} %add.440), channel_id=1, source_target_pairs={{0,8},{1,5},{2,10},{3,7},{4,12},{5,1},{6,14},{7,3},{8,0},{9,13},{1... | collective-permute-start | bytes 884744 | tf_op jit(solution)/shard_map/ppermute | solution.py:40
  57.2 7.0 %collective-permute-start.5 = (bf16[32,2304]{1,0:T(8,128)(2,1)S(1)}, bf16[32,2304]{1,0:T(8,128)(2,1)S(1)}, u32[]{:S(2)}, u32[]{:S(2)}) collective-permute-start(bf16[32,2304]{1,0:T(8,128)(2,1)S(1)} %get-tuple-element.23), channel_id=1, source_target_pairs={{0,32},{32,64},{64,96},{1,33},{33,65},{65,97},{2,34},{34,66},{66,9... | collective-permute-start | bytes 442376 | tf_op jit(solution)/shard_map/ppermute | solution.py:19
  81.8 9.4 %collective-permute-start.7 = (f32[32,2304]{1,0:T(8,128)S(1)}, f32[32,2304]{1,0:T(8,128)S(1)}, u32[]{:S(2)}, u32[]{:S(2)}) collective-permute-start(f32[32,2304]{1,0:T(8,128)S(1)} %dynamic-slice_bitcast_fusion.12), channel_id=1, source_target_pairs={{0,2},{1,3},{2,0},{3,1},{4,6},{5,7},{6,4},{7,5},{8,10},{9,11},{10,... | collective-permute-start | bytes 884744 | tf_op jit(solution)/shard_map/ppermute | solution.py:24
  91.2 8.3 %collective-permute-start.8 = (f32[32,2304]{1,0:T(8,128)S(1)}, f32[32,2304]{1,0:T(8,128)S(1)}, u32[]{:S(2)}, u32[]{:S(2)}) collective-permute-start(f32[32,2304]{1,0:T(8,128)S(1)} %bitcast_add_fusion.12), channel_id=1, source_target_pairs={{0,16},{1,9},{2,18},{3,11},{4,20},{5,13},{6,22},{7,15},{8,24},{9,1... | collective-permute-start | bytes 884744 | tf_op jit(solution)/shard_map/ppermute | solution.py:40
  99.5 6.8 %collective-permute-start.9 = (f32[32,2304]{1,0:T(8,128)S(1)}, f32[32,2304]{1,0:T(8,128)S(1)}, u32[]{:S(2)}, u32[]{:S(2)}) collective-permute-start(f32[32,2304]{1,0:T(8,128)S(1)} %add.452), channel_id=1, source_target_pairs={{0,4},{1,17},{2,6},{3,19},{4,0},{5,21},{6,2},{7,23},{8,12},{9,25},... | collective-permute-start | bytes 884744 | tf_op jit(solution)/shard_map/ppermute | solution.py:40
  106.4 8.6 %collective-permute-start.10 = (f32[32,2304]{1,0:T(8,128)S(1)}, f32[32,2304]{1,0:T(8,128)S(1)}, u32[]{:S(2)}, u32[]{:S(2)}) collective-permute-start(f32[32,2304]{1,0:T(8,128)S(1)} %add.453), channel_id=1, source_target_pairs={{0,8},{1,5},{2,10},{3,7},{4,12},{5,1},{6,14},{7,3},{8,0},{9,13},{1... | collective-permute-start | bytes 884744 | tf_op jit(solution)/shard_map/ppermute | solution.py:40
  115.1 7.0 %collective-permute-start.11 = (bf16[32,2304]{1,0:T(8,128)(2,1)S(1)}, bf16[32,2304]{1,0:T(8,128)(2,1)S(1)}, u32[]{:S(2)}, u32[]{:S(2)}) collective-permute-start(bf16[32,2304]{1,0:T(8,128)(2,1)S(1)} %get-tuple-element.19), channel_id=1, source_target_pairs={{0,32},{32,64},{64,96},{1,33},{33,65},{65,97},{2,34},{34,66},{66,9... | collective-permute-start | bytes 442376 | tf_op jit(solution)/shard_map/ppermute | solution.py:19
  140.1 9.3 %collective-permute-start.13 = (f32[32,2304]{1,0:T(8,128)S(1)}, f32[32,2304]{1,0:T(8,128)S(1)}, u32[]{:S(2)}, u32[]{:S(2)}) collective-permute-start(f32[32,2304]{1,0:T(8,128)S(1)} %dynamic-slice_bitcast_fusion.11), channel_id=1, source_target_pairs={{0,2},{1,3},{2,0},{3,1},{4,6},{5,7},{6,4},{7,5},{8,10},{9,11},{10,... | collective-permute-start | bytes 884744 | tf_op jit(solution)/shard_map/ppermute | solution.py:24
  149.4 8.3 %collective-permute-start.14 = (f32[32,2304]{1,0:T(8,128)S(1)}, f32[32,2304]{1,0:T(8,128)S(1)}, u32[]{:S(2)}, u32[]{:S(2)}) collective-permute-start(f32[32,2304]{1,0:T(8,128)S(1)} %bitcast_add_fusion.11), channel_id=1, source_target_pairs={{0,16},{1,9},{2,18},{3,11},{4,20},{5,13},{6,22},{7,15},{8,24},{9,1... | collective-permute-start | bytes 884744 | tf_op jit(solution)/shard_map/ppermute | solution.py:40
  157.8 6.8 %collective-permute-start.15 = (f32[32,2304]{1,0:T(8,128)S(1)}, f32[32,2304]{1,0:T(8,128)S(1)}, u32[]{:S(2)}, u32[]{:S(2)}) collective-permute-start(f32[32,2304]{1,0:T(8,128)S(1)} %add.463), channel_id=1, source_target_pairs={{0,4},{1,17},{2,6},{3,19},{4,0},{5,21},{6,2},{7,23},{8,12},{9,25},... | collective-permute-start | bytes 884744 | tf_op jit(solution)/shard_map/ppermute | solution.py:40
  164.6 9.5 %collective-permute-start.16 = (f32[32,2304]{1,0:T(8,128)S(1)}, f32[32,2304]{1,0:T(8,128)S(1)}, u32[]{:S(2)}, u32[]{:S(2)}) collective-permute-start(f32[32,2304]{1,0:T(8,128)S(1)} %add.464), channel_id=1, source_target_pairs={{0,8},{1,5},{2,10},{3,7},{4,12},{5,1},{6,14},{7,3},{8,0},{9,13},{1... | collective-permute-start | bytes 884744 | tf_op jit(solution)/shard_map/ppermute | solution.py:40
  174.2 7.0 %collective-permute-start.17 = (bf16[32,2304]{1,0:T(8,128)(2,1)S(1)}, bf16[32,2304]{1,0:T(8,128)(2,1)S(1)}, u32[]{:S(2)}, u32[]{:S(2)}) collective-permute-start(bf16[32,2304]{1,0:T(8,128)(2,1)S(1)} %get-tuple-element.15), channel_id=1, source_target_pairs={{0,32},{32,64},{64,96},{1,33},{33,65},{65,97},{2,34},{34,66},{66,9... | collective-permute-start | bytes 442376 | tf_op jit(solution)/shard_map/ppermute | solution.py:19
  198.9 9.3 %collective-permute-start.19 = (f32[32,2304]{1,0:T(8,128)S(1)}, f32[32,2304]{1,0:T(8,128)S(1)}, u32[]{:S(2)}, u32[]{:S(2)}) collective-permute-start(f32[32,2304]{1,0:T(8,128)S(1)} %dynamic-slice_bitcast_fusion.10), channel_id=1, source_target_pairs={{0,2},{1,3},{2,0},{3,1},{4,6},{5,7},{6,4},{7,5},{8,10},{9,11},{10,... | collective-permute-start | bytes 884744 | tf_op jit(solution)/shard_map/ppermute | solution.py:24
  208.3 8.3 %collective-permute-start.20 = (f32[32,2304]{1,0:T(8,128)S(1)}, f32[32,2304]{1,0:T(8,128)S(1)}, u32[]{:S(2)}, u32[]{:S(2)}) collective-permute-start(f32[32,2304]{1,0:T(8,128)S(1)} %bitcast_add_fusion.10), channel_id=1, source_target_pairs={{0,16},{1,9},{2,18},{3,11},{4,20},{5,13},{6,22},{7,15},{8,24},{9,1... | collective-permute-start | bytes 884744 | tf_op jit(solution)/shard_map/ppermute | solution.py:40
  216.6 6.8 %collective-permute-start.21 = (f32[32,2304]{1,0:T(8,128)S(1)}, f32[32,2304]{1,0:T(8,128)S(1)}, u32[]{:S(2)}, u32[]{:S(2)}) collective-permute-start(f32[32,2304]{1,0:T(8,128)S(1)} %add.474), channel_id=1, source_target_pairs={{0,4},{1,17},{2,6},{3,19},{4,0},{5,21},{6,2},{7,23},{8,12},{9,25},... | collective-permute-start | bytes 884744 | tf_op jit(solution)/shard_map/ppermute | solution.py:40
  223.5 8.6 %collective-permute-start.22 = (f32[32,2304]{1,0:T(8,128)S(1)}, f32[32,2304]{1,0:T(8,128)S(1)}, u32[]{:S(2)}, u32[]{:S(2)}) collective-permute-start(f32[32,2304]{1,0:T(8,128)S(1)} %add.475), channel_id=1, source_target_pairs={{0,8},{1,5},{2,10},{3,7},{4,12},{5,1},{6,14},{7,3},{8,0},{9,13},{1... | collective-permute-start | bytes 884744 | tf_op jit(solution)/shard_map/ppermute | solution.py:40
  232.2 7.3 %collective-permute-start.23 = (bf16[32,2304]{1,0:T(8,128)(2,1)S(1)}, bf16[32,2304]{1,0:T(8,128)(2,1)S(1)}, u32[]{:S(2)}, u32[]{:S(2)}) collective-permute-start(bf16[32,2304]{1,0:T(8,128)(2,1)S(1)} %get-tuple-element.11), channel_id=1, source_target_pairs={{0,32},{32,64},{64,96},{1,33},{33,65},{65,97},{2,34},{34,66},{66,9... | collective-permute-start | bytes 442376 | tf_op jit(solution)/shard_map/ppermute | solution.py:19
  257.3 9.3 %collective-permute-start.25 = (f32[32,2304]{1,0:T(8,128)S(1)}, f32[32,2304]{1,0:T(8,128)S(1)}, u32[]{:S(2)}, u32[]{:S(2)}) collective-permute-start(f32[32,2304]{1,0:T(8,128)S(1)} %dynamic-slice_bitcast_fusion.9), channel_id=1, source_target_pairs={{0,2},{1,3},{2,0},{3,1},{4,6},{5,7},{6,4},{7,5},{8,10},{9,11},{10,... | collective-permute-start | bytes 884744 | tf_op jit(solution)/shard_map/ppermute | solution.py:24
  266.7 8.3 %collective-permute-start.26 = (f32[32,2304]{1,0:T(8,128)S(1)}, f32[32,2304]{1,0:T(8,128)S(1)}, u32[]{:S(2)}, u32[]{:S(2)}) collective-permute-start(f32[32,2304]{1,0:T(8,128)S(1)} %bitcast_add_fusion.9), channel_id=1, source_target_pairs={{0,16},{1,9},{2,18},{3,11},{4,20},{5,13},{6,22},{7,15},{8,24},{9,1... | collective-permute-start | bytes 884744 | tf_op jit(solution)/shard_map/ppermute | solution.py:40
  281.9 9.5 %collective-permute-start.28 = (f32[32,2304]{1,0:T(8,128)S(1)}, f32[32,2304]{1,0:T(8,128)S(1)}, u32[]{:S(2)}, u32[]{:S(2)}) collective-permute-start(f32[32,2304]{1,0:T(8,128)S(1)} %add.486), channel_id=1, source_target_pairs={{0,8},{1,5},{2,10},{3,7},{4,12},{5,1},{6,14},{7,3},{8,0},{9,13},{1... | collective-permute-start | bytes 884744 | tf_op jit(solution)/shard_map/ppermute | solution.py:40
  291.4 7.3 %collective-permute-start.29 = (bf16[32,2304]{1,0:T(8,128)(2,1)S(1)}, bf16[32,2304]{1,0:T(8,128)(2,1)S(1)}, u32[]{:S(2)}, u32[]{:S(2)}) collective-permute-start(bf16[32,2304]{1,0:T(8,128)(2,1)S(1)} %get-tuple-element.9), channel_id=1, source_target_pairs={{0,32},{32,64},{64,96},{1,33},{33,65},{65,97},{2,34},{34,66},{66,9... | collective-permute-start | bytes 442376 | tf_op jit(solution)/shard_map/ppermute | solution.py:19
  317.8 9.6 %collective-permute-start.31 = (f32[32,2304]{1,0:T(8,128)}, f32[32,2304]{1,0:T(8,128)}, u32[]{:S(2)}, u32[]{:S(2)}) collective-permute-start(f32[32,2304]{1,0:T(8,128)} %dynamic-slice_bitcast_fusion.8), channel_id=1, source_target_pairs={{0,2},{1,3},{2,0},{3,1},{4,6},{5,7},{6,4},{7,5},{8,10},{9,11},{10,... | collective-permute-start | bytes 884744 | tf_op jit(solution)/shard_map/ppermute | solution.py:24
  329.1 8.5 %collective-permute-start.32 = (f32[32,2304]{1,0:T(8,128)}, f32[32,2304]{1,0:T(8,128)}, u32[]{:S(2)}, u32[]{:S(2)}) collective-permute-start(f32[32,2304]{1,0:T(8,128)} %bitcast_add_fusion.8), channel_id=1, source_target_pairs={{0,16},{1,9},{2,18},{3,11},{4,20},{5,13},{6,22},{7,15},{8,24},{9,1... | collective-permute-start | bytes 884744 | tf_op jit(solution)/shard_map/ppermute | solution.py:40
  338.7 6.8 %collective-permute-start.33 = (f32[32,2304]{1,0:T(8,128)S(1)}, f32[32,2304]{1,0:T(8,128)S(1)}, u32[]{:S(2)}, u32[]{:S(2)}) collective-permute-start(f32[32,2304]{1,0:T(8,128)S(1)} %add.496), channel_id=1, source_target_pairs={{0,4},{1,17},{2,6},{3,19},{4,0},{5,21},{6,2},{7,23},{8,12},{9,25},... | collective-permute-start | bytes 884744 | tf_op jit(solution)/shard_map/ppermute | solution.py:40
  345.6 8.8 %collective-permute-start.34 = (f32[32,2304]{1,0:T(8,128)S(1)}, f32[32,2304]{1,0:T(8,128)S(1)}, u32[]{:S(2)}, u32[]{:S(2)}) collective-permute-start(f32[32,2304]{1,0:T(8,128)S(1)} %add.497), channel_id=1, source_target_pairs={{0,8},{1,5},{2,10},{3,7},{4,12},{5,1},{6,14},{7,3},{8,0},{9,13},{1... | collective-permute-start | bytes 884744 | tf_op jit(solution)/shard_map/ppermute | solution.py:40
  354.6 7.0 %collective-permute-start.35 = (bf16[32,2304]{1,0:T(8,128)(2,1)S(1)}, bf16[32,2304]{1,0:T(8,128)(2,1)S(1)}, u32[]{:S(2)}, u32[]{:S(2)}) collective-permute-start(bf16[32,2304]{1,0:T(8,128)(2,1)S(1)} %get-tuple-element.7), channel_id=1, source_target_pairs={{0,32},{32,64},{64,96},{1,33},{33,65},{65,97},{2,34},{34,66},{66,9... | collective-permute-start | bytes 442376 | tf_op jit(solution)/shard_map/ppermute | solution.py:19
  378.2 9.3 %collective-permute-start.37 = (f32[32,2304]{1,0:T(8,128)S(1)}, f32[32,2304]{1,0:T(8,128)S(1)}, u32[]{:S(2)}, u32[]{:S(2)}) collective-permute-start(f32[32,2304]{1,0:T(8,128)S(1)} %dynamic-slice_bitcast_fusion.7), channel_id=1, source_target_pairs={{0,2},{1,3},{2,0},{3,1},{4,6},{5,7},{6,4},{7,5},{8,10},{9,11},{10,... | collective-permute-start | bytes 884744 | tf_op jit(solution)/shard_map/ppermute | solution.py:24
  387.6 8.3 %collective-permute-start.38 = (f32[32,2304]{1,0:T(8,128)S(1)}, f32[32,2304]{1,0:T(8,128)S(1)}, u32[]{:S(2)}, u32[]{:S(2)}) collective-permute-start(f32[32,2304]{1,0:T(8,128)S(1)} %bitcast_add_fusion.7), channel_id=1, source_target_pairs={{0,16},{1,9},{2,18},{3,11},{4,20},{5,13},{6,22},{7,15},{8,24},{9,1... | collective-permute-start | bytes 884744 | tf_op jit(solution)/shard_map/ppermute | solution.py:40
  402.8 9.5 %collective-permute-start.40 = (f32[32,2304]{1,0:T(8,128)S(1)}, f32[32,2304]{1,0:T(8,128)S(1)}, u32[]{:S(2)}, u32[]{:S(2)}) collective-permute-start(f32[32,2304]{1,0:T(8,128)S(1)} %add.508), channel_id=1, source_target_pairs={{0,8},{1,5},{2,10},{3,7},{4,12},{5,1},{6,14},{7,3},{8,0},{9,13},{1... | collective-permute-start | bytes 884744 | tf_op jit(solution)/shard_map/ppermute | solution.py:40
  (54 other events, 418.6 us)
